TPU v7x, 256 devices: a whole 4x4x8 slice. The times are simulated.
256 devices in a mesh: expert: 64 (over y, z, core), tensor: 4 (over x).
Axes of the slice: x: 4, y: 4, z: 8, core: 2. Of those that a mesh axis runs over, the one named last changes fastest.
Arguments:
- tokens: bfloat16 [8192, 2048], P('expert', 'tensor'), may hold values from -6 to 6
- labels: int32 [8192, 1], P('expert'), may hold values from 0 to 31, as said below
- domain_ids: int32 [8192], P('expert'), may hold values from 0 to 21
- domain_weights: float32 [22], replicated, may hold values from 0.02 to 0.5
- cotangent: bfloat16 [8192, 2048], P('expert', 'tensor'), may hold values from -6 to 6
- gate_weight: bfloat16 [64, 2048, 2048], P('expert', None, 'tensor'), may hold values from -0.125 to 0.125
- up_weight: bfloat16 [64, 2048, 2048], P('expert', None, 'tensor'), may hold values from -0.125 to 0.125
- down_weight: bfloat16 [64, 2048, 2048], P('expert', 'tensor'), may hold values from -0.09375 to 0.09375
Outputs:
- layer_out: bfloat16 [8192, 2048], P('expert', 'tensor')
- input_grad: bfloat16 [8192, 2048], P('expert', 'tensor')
- gate_grad: bfloat16 [64, 2048, 2048], P('expert', None, 'tensor')
- up_grad: bfloat16 [64, 2048, 2048], P('expert', None, 'tensor')
- down_grad: bfloat16 [64, 2048, 2048], P('expert', 'tensor')
Inputs may be any that keep to these rules, and one draw needn't show every extreme that they name: `labels`: among the rows of one device (aligned blocks of 128 rows) no label appears more than 8 times, and every such block has some label exactly 8 times.
All inputs are finite; a program needn't handle non-finite values.
Results may differ from a plain program's by a relative error of at most 0.0058.
Values may be sent and summed in bfloat16 or wider, within the bound.
No kernel may reach another device: no remote copies, remote signals or barrier semaphores. Data moves between devices by JAX's collectives and lax.ppermute only.
A program may use at most 320 MiB of HBM per device.

v0:
```python
import jax
import jax.numpy as jnp
from jax import lax
from jax.sharding import PartitionSpec as P

SPLIT = 2


def partner(value, axis, stride):
    return lax.ppermute(value, axis, [(i, i ^ 1 << stride) for i in range(lax.axis_size(axis))])


def silu_parts(gate_pre):
    squash = jax.nn.sigmoid(gate_pre)
    return (squash, gate_pre * squash)


def body(
    tokens, labels, domain_ids, domain_weights, cotangent, gate_weight, up_weight, down_weight
):
    n_expert = lax.axis_size("expert")
    tok_rows = tokens.shape[0]
    experts_all = n_expert // SPLIT
    capacity = 2 * tok_rows // experts_all
    half_cap = capacity // 2
    parity = lax.axis_index("expert") % 2
    lang_label = labels[:, 0]
    dom_hot = (
        domain_ids[:, None] == jnp.arange(domain_weights.shape[0], dtype=jnp.int32)[None, :]
    ).astype(jnp.float32)
    tok_scale = jnp.sum(dom_hot * domain_weights[None, :], axis=1)
    grad_rows = (tok_scale[:, None] * cotangent.astype(jnp.float32)).astype(jnp.bfloat16)
    lab_hot = (lang_label[:, None] == jnp.arange(experts_all, dtype=jnp.int32)[None, :]).astype(
        jnp.float32
    )
    row_ids = jnp.arange(tok_rows, dtype=jnp.int32)
    earlier = (row_ids[None, :] < row_ids[:, None]).astype(jnp.float32)
    before = jnp.dot(earlier, lab_hot, precision=lax.Precision.HIGHEST)
    slot_pos = jnp.sum(before * lab_hot, axis=1).astype(jnp.int32)
    target_row = lang_label * capacity + slot_pos
    sources = jnp.stack((tokens, grad_rows))
    sources = lax.all_gather(sources, "tensor", axis=2, tiled=True)
    slot_ids = jnp.arange(n_expert * capacity, dtype=jnp.int32)
    dispatch_map = (slot_ids[:, None] // capacity // SPLIT == lang_label[None, :]) & (
        slot_ids[:, None] % capacity == slot_pos[None, :]
    )
    dispatch_map = dispatch_map.astype(jnp.bfloat16)
    outbound = jnp.einsum(
        "rt,ktw->krw", dispatch_map, sources, preferred_element_type=jnp.float32
    ).astype(jnp.bfloat16)
    outbound = outbound.reshape(2, n_expert, capacity, sources.shape[2])
    arrived = lax.all_to_all(outbound, "expert", split_axis=1, concat_axis=1, tiled=True)
    rows_all = n_expert * capacity
    feat_width = arrived.shape[3]
    routed = arrived[0].reshape(rows_all, feat_width)
    routed_grad = arrived[1].reshape(rows_all, feat_width)
    w_gate = gate_weight[0]
    w_up = up_weight[0]
    w_down = down_weight[0]
    contract_rows = (((0,), (0,)), ((), ()))
    contract_cols = (((1,), (1,)), ((), ()))
    gate_pre = jnp.dot(routed, w_gate, preferred_element_type=jnp.float32)
    up_pre = jnp.dot(routed, w_up, preferred_element_type=jnp.float32)
    squash, activated = silu_parts(gate_pre)
    hidden = (activated * up_pre).astype(jnp.bfloat16)
    out_part = jnp.dot(hidden, w_down, preferred_element_type=jnp.float32)
    grad_hidden = lax.dot_general(
        routed_grad, w_down, contract_cols, preferred_element_type=jnp.float32
    )
    grad_gate_pre = (grad_hidden * up_pre * squash * (1.0 + gate_pre * (1.0 - squash))).astype(
        jnp.bfloat16
    )
    grad_up_pre = (grad_hidden * activated).astype(jnp.bfloat16)
    gate_grad = lax.dot_general(
        routed, grad_gate_pre, contract_rows, preferred_element_type=jnp.float32
    ).astype(jnp.bfloat16)[None]
    up_grad = lax.dot_general(
        routed, grad_up_pre, contract_rows, preferred_element_type=jnp.float32
    ).astype(jnp.bfloat16)[None]
    down_grad = lax.dot_general(
        hidden, routed_grad, contract_rows, preferred_element_type=jnp.float32
    ).astype(jnp.bfloat16)[None]
    input_part = lax.dot_general(
        grad_gate_pre, w_gate, contract_cols, preferred_element_type=jnp.float32
    ) + lax.dot_general(grad_up_pre, w_up, contract_cols, preferred_element_type=jnp.float32)
    out_part = out_part.reshape(n_expert, capacity, feat_width)
    input_part = input_part.reshape(n_expert, capacity, feat_width)
    out_share, input_share = (
        lax.psum_scatter(out_part, "tensor", scatter_dimension=2, tiled=True),
        lax.psum_scatter(input_part, "tensor", scatter_dimension=2, tiled=True),
    )
    partial_value = jnp.stack((out_share, input_share))
    kept = jnp.where(parity == 0, partial_value[:, :, :half_cap], partial_value[:, :, half_cap:])
    handed = jnp.where(parity == 0, partial_value[:, :, half_cap:], partial_value[:, :, :half_cap])
    summed = kept + partner(handed, "expert", 0)
    going_back = summed.astype(jnp.bfloat16)
    returned = lax.all_to_all(going_back, "expert", split_axis=1, concat_axis=1, tiled=True)
    home_ids = jnp.arange(n_expert * half_cap, dtype=jnp.int32)
    home_map = (home_ids[:, None] == target_row[None, :]).astype(jnp.bfloat16)
    flat_back = returned.reshape(2, n_expert * half_cap, returned.shape[3])
    gathered_home = jnp.einsum(
        "rt,krw->ktw", home_map, flat_back, preferred_element_type=jnp.float32
    ).astype(jnp.bfloat16)
    return (gathered_home[0], gathered_home[1], gate_grad, up_grad, down_grad)


def solution(mesh):
    return jax.shard_map(
        body,
        mesh=mesh,
        in_specs=(
            P("expert", "tensor"),
            P("expert", None),
            P("expert"),
            P(),
            P("expert", "tensor"),
            P("expert", None, "tensor"),
            P("expert", None, "tensor"),
            P("expert", "tensor", None),
        ),
        out_specs=(
            P("expert", "tensor"),
            P("expert", "tensor"),
            P("expert", None, "tensor"),
            P("expert", None, "tensor"),
            P("expert", "tensor", None),
        ),
        check_vma=False,
    )
```

profile of v0, /device:TPU:1, one launch (start us, length us, event | category | flops | bytes accessed | tf_op | source)
XLA Modules:
  0.0 302.7 jit_solution(17173675187760145169)
XLA Ops:
  7.2 0.9 select_reduce_fusion
  8.1 1.0 fusion.24
  9.1 1.6 pad_maximum_fusion.1
  10.8 0.9 fusion.15
  11.7 28.7 %all-gather.2.cloned.1.call-done = bf16[2,128,2048]{2,1,0:T(8,128)(2,1)} async-done(((bf16[2,128,512]{2,1,0:T(8,128)(2,1)}), bf16[2,128,2048]{2,1,0:T(8,128)(2,1)}) %all-gather.2.cloned.1.call-update) | async-done | bytes 1048592 | tf_op jit(solution)/shard_map/all_gather | solution.py:42
  40.4 2.5 convert_bitcast_fusion
  43.5 107.7 %all_to_all.10 = bf16[2,64,8,2048]{3,2,0,1:T(8,128)(2,1)S(1)} all-to-all(bf16[2,64,8,2048]{3,2,0,1:T(8,128)(2,1)S(1)} %copy.27), channel_id=1, replica_groups=mesh['expert'=64,'tensor'=4] {'expert'}, dimensions={1} | all-to-all | bytes 8388608 | tf_op jit(solution)/shard_map/all_to_all | solution.py:52
  151.3 1.2 fusion.12
  152.5 1.9 copy-done.5
  154.4 1.3 fusion.5
  155.7 1.6 multiply_convert_fusion.2
  157.3 1.3 fusion.10
  158.7 3.3 %add_bitcast_fusion = f32[64,8,2048]{2,1,0:T(8,128)} fusion(f32[512,2048]{1,0:T(8,128)S(1)} %fusion.10, bf16[512,512]{1,0:T(8,128)(2,1)S(1)} %get-tuple-element.27, bf16[1,2048,512]{2,1,0:T(8,128)(2,1)S(1)} %copy-done), kind=kOutput, calls=%fused_computation | convolution fusion | flops 1074790400 | bytes 11010048 | tf_op jit(solution)/shard_map/dot_general | solution.py:85
  162.0 4.8 %fusion.3 = f32[64,8,2048]{2,1,0:T(8,128)} fusion(bf16[1,512,2048]{2,1,0:T(8,128)(2,1)} %param.15, bf16[512,512]{1,0:T(8,128)(2,1)S(1)} %get-tuple-element.25), kind=kOutput, calls=%fused_computation.12 | convolution fusion | flops 1073741824 | bytes 6815744 | tf_op jit(solution)/shard_map/dot_general | solution.py:66
  166.9 40.1 %reduce-scatter.5.cloned.1.call-done = f32[64,8,512]{2,1,0:T(8,128)} async-done(((f32[64,8,2048]{2,1,0:T(8,128)}), f32[64,8,512]{2,1,0:T(8,128)}) %reduce-scatter.5.cloned.1.call-update) | async-done | bytes 1048592 | tf_op jit(solution)/shard_map/reduce_scatter | solution.py:90
  207.0 51.8 %reduce-scatter.3.cloned.1.call-done = f32[64,8,512]{2,1,0:T(8,128)} async-done(((f32[64,8,2048]{2,1,0:T(8,128)}), f32[64,8,512]{2,1,0:T(8,128)}) %reduce-scatter.3.cloned.1.call-update) | async-done | bytes 1048592 | tf_op jit(solution)/shard_map/reduce_scatter | solution.py:89
  258.8 2.8 broadcast_select_fusion
  262.4 2.3 collective-permute-done
  265.1 1.0 copy.28
  266.1 10.4 %all-to-all-start.1 = ((bf16[2,64,4,512]{3,2,0,1:T(4,128)(2,1)}), bf16[2,64,4,512]{3,2,0,1:T(4,128)(2,1)S(1)}, u32[]{:S(2)}, u32[]{:S(2)}) async-start(bf16[2,64,4,512]{3,2,0,1:T(4,128)(2,1)} %copy.28), calls=%async_computation.3 | async-start | bytes 1048576 | tf_op jit(solution)/shard_map/all_to_all | solution.py:97
  276.5 4.5 %fusion.2 = bf16[1,512,2048]{2,1,0:T(8,128)(2,1)} fusion(bf16[512,512]{1,0:T(8,128)(2,1)} %copy-done.9, bf16[2,64,8,2048]{3,2,0,1:T(8,128)(2,1)} %copy-done.1), kind=kOutput, calls=%fused_computation.7 | convolution fusion | flops 1074790400 | bytes 4718592 | tf_op jit(solution)/shard_map/dot_general | solution.py:80
  281.0 2.6 fusion
  283.7 2.6 fusion.1
  286.3 7.5 %all-to-all-done.1 = bf16[2,64,4,512]{3,2,0,1:T(4,128)(2,1)S(1)} async-done(((bf16[2,64,4,512]{3,2,0,1:T(4,128)(2,1)}), bf16[2,64,4,512]{3,2,0,1:T(4,128)(2,1)S(1)}, u32[]{:S(2)}, u32[]{:S(2)}) %all-to-all-start.1) | async-done | bytes 524320 | tf_op jit(solution)/shard_map/all_to_all | solution.py:97
  (42 shorter events, 4.3 us)
Async XLA Ops:
  7.2 148.5 %copy-start = (bf16[1,2048,512]{2,1,0:T(8,128)(2,1)S(1)}, bf16[1,2048,512]{2,1,0:T(8,128)(2,1)}, u32[]{:S(2)}) copy-start(bf16[1,2048,512]{2,1,0:T(8,128)(2,1)} %param.14) | copy-start | bytes 6291460
  7.2 33.2 %all-gather.2.cloned.1.call-start = ((), (), s32[]{:S(2)}) async-start(), calls=%async_computation.4 | async-start | bytes 1310720 | tf_op jit(solution)/shard_map/all_gather | solution.py:42
  10.8 196.2 %reduce-scatter.5.cloned.1.call-start = ((), (), s32[]{:S(2)}) async-start(), calls=%async_computation.6 | async-start | bytes 5242880 | tf_op jit(solution)/shard_map/reduce_scatter | solution.py:90
  43.5 107.7 %copy-start.6 = (bf16[1,2048,512]{2,1,0:T(8,128)(2,1)S(1)}, bf16[1,2048,512]{2,1,0:T(8,128)(2,1)}, u32[]{:S(2)}) copy-start(bf16[1,2048,512]{2,1,0:T(8,128)(2,1)} %param.13) | copy-start | bytes 6291460
  151.2 4.4 %copy-start.1 = (bf16[2,64,8,2048]{3,2,0,1:T(8,128)(2,1)}, bf16[2,64,8,2048]{3,2,0,1:T(8,128)(2,1)S(1)}, u32[]{:S(2)}) copy-start(bf16[2,64,8,2048]{3,2,0,1:T(8,128)(2,1)S(1)} %all_to_all.10) | copy-start | bytes 12582916
  151.2 3.1 %copy-start.5 = (bf16[1,512,2048]{2,1,0:T(8,128)(2,1)S(1)}, bf16[1,512,2048]{2,1,0:T(8,128)(2,1)}, u32[]{:S(2)}) copy-start(bf16[1,512,2048]{2,1,0:T(8,128)(2,1)} %param.15) | copy-start | bytes 6291460
  157.3 1.3 copy-start.7
  157.3 1.3 copy-start.10
  157.3 4.7 %copy-start.9 = (bf16[512,512]{1,0:T(8,128)(2,1)}, bf16[512,512]{1,0:T(8,128)(2,1)S(1)}, u32[]{:S(2)}) copy-start(bf16[512,512]{1,0:T(8,128)(2,1)S(1)} %get-tuple-element.25) | copy-start | bytes 1572868
  161.9 96.9 %reduce-scatter.3.cloned.1.call-start = ((), (), s32[]{:S(2)}) async-start(), calls=%async_computation.5 | async-start | bytes 5242880 | tf_op jit(solution)/shard_map/reduce_scatter | solution.py:89
  207.0 57.7 %copy-start.3 = (f32[64,8,512]{2,1,0:T(8,128)S(1)}, f32[64,8,512]{2,1,0:T(8,128)}, u32[]{:S(2)}) copy-start(f32[64,8,512]{2,1,0:T(8,128)} %reduce-scatter.5.cloned.1.call-done) | copy-start | bytes 3145732
  258.8 5.8 %copy-start.4 = (f32[64,8,512]{2,1,0:T(8,128)S(1)}, f32[64,8,512]{2,1,0:T(8,128)}, u32[]{:S(2)}) copy-start(f32[64,8,512]{2,1,0:T(8,128)} %reduce-scatter.3.cloned.1.call-done) | copy-start | bytes 3145732
  261.6 14.8 %copy-start.12 = (s32[128,1]{0,1:T(1,128)S(1)}, s32[128,1]{0,1:T(1,128)}, u32[]{:S(2)}) copy-start(s32[128,1]{0,1:T(1,128)} %param.9) | copy-start | bytes 1540
  261.7 3.0 collective-permute-start
  266.1 27.7 %all-to-all-start.1 = ((bf16[2,64,4,512]{3,2,0,1:T(4,128)(2,1)}), bf16[2,64,4,512]{3,2,0,1:T(4,128)(2,1)S(1)}, u32[]{:S(2)}, u32[]{:S(2)}) async-start(bf16[2,64,4,512]{3,2,0,1:T(4,128)(2,1)} %copy.28), calls=%async_computation.3 | async-start | bytes 1048576 | tf_op jit(solution)/shard_map/all_to_all | solution.py:97
  276.5 4.5 %copy-start.2 = (bf16[2,64,8,2048]{3,2,0,1:T(8,128)(2,1)S(1)}, bf16[2,64,8,2048]{3,2,0,1:T(8,128)(2,1)}, u32[]{:S(2)}) copy-start(bf16[2,64,8,2048]{3,2,0,1:T(8,128)(2,1)} %copy-done.1) | copy-start | bytes 12582916
  276.5 4.5 %copy-start.8 = (bf16[512,512]{1,0:T(8,128)(2,1)S(1)}, bf16[512,512]{1,0:T(8,128)(2,1)}, u32[]{:S(2)}) copy-start(bf16[512,512]{1,0:T(8,128)(2,1)} %copy-done.7) | copy-start | bytes 1572868
  281.0 2.6 copy-start.11
Sparse Core Ops, SparseCore 0:
  10.9 29.4 all-gather.1
  162.1 44.8 reduce-scatter.4
  209.7 49.0 reduce-scatter.2
where the time goes:
time: 303 us
  waiting for transfers between devices  130 us (43%)
  blocking collectives  108 us (36%)
  matrix products  27 us (9%)
  between operations  14 us (5%)
  starting transfers between devices  11.2 us (4%)
  other arithmetic  6.76 us (2%)
  local copies, waits for them, and re-layouts  5.46 us (2%)
    all_to_all x1, blocking collectives, body(): lax.all_to_all(outbound, 'expert', split_axis=1, concat_axis=1, tiled=True)  108 us
    reduce_scatter x1, waiting for transfers between devices, body(): lax.psum_scatter(out_part, 'tensor', scatter_dimension=2, tiled=True)  51.8 us
    reduce_scatter x1, waiting for transfers between devices, body(): lax.psum_scatter(input_part, 'tensor', scatter_dimension=2, tiled=True)  40.1 us
    all_gather x1, waiting for transfers between devices, body(): sources = lax.all_gather(sources, 'tensor', axis=2, tiled=True)  28.7 us
    all_to_all x1, starting transfers between devices, body(): lax.all_to_all(going_back, 'expert', split_axis=1, concat_axis=1, tiled=T...  10.4 us
    all_to_all x1, waiting for transfers between devices, body(): lax.all_to_all(going_back, 'expert', split_axis=1, concat_axis=1, tiled=T...  7.52 us
  transfers between devices with their start and end apart: 5, of which 5 were waited for; matrix products, arithmetic and copies ran while one was open for 5% of the time, Pallas kernels for 0%

commit v1 on v0

--- a/solution.py
+++ b/solution.py
@@ -39,7 +39,10 @@
     slot_pos = jnp.sum(before * lab_hot, axis=1).astype(jnp.int32)
     target_row = lang_label * capacity + slot_pos
     sources = jnp.stack((tokens, grad_rows))
-    sources = lax.all_gather(sources, "tensor", axis=2, tiled=True)
+    n_dev = lax.axis_size("tensor")
+    blocks = jnp.stack([sources for _ in range(n_dev)])
+    blocks = lax.all_to_all(blocks, "tensor", split_axis=0, concat_axis=0)
+    sources = jnp.concatenate(blocks, axis=2)
     slot_ids = jnp.arange(n_expert * capacity, dtype=jnp.int32)
     dispatch_map = (slot_ids[:, None] // capacity // SPLIT == lang_label[None, :]) & (
         slot_ids[:, None] % capacity == slot_pos[None, :]

time: 303 us -> 293 us (0.967)
  waiting for transfers between devices: 130 us -> 114 us
  starting transfers between devices: 11.2 us -> 16 us
    all_gather x1 -> x0, waiting for transfers between devices: 28.7 us -> none  [body(): sources = lax.all_gather(sources, 'tensor', axis=2, tiled=True)]
    all_to_all x0 -> x1, waiting for transfers between devices: none -> 13.1 us  [body(): blocks = lax.all_to_all(blocks, 'tensor', split_axis=0, concat_axis=0)]
    all_to_all x0 -> x1, starting transfers between devices: none -> 4.84 us  [body(): blocks = lax.all_to_all(blocks, 'tensor', split_axis=0, concat_axis=0)]
where the time goes in v1:
time: 293 us
  waiting for transfers between devices  114 us (39%)
  blocking collectives  111 us (38%)
  matrix products  25.1 us (9%)
  starting transfers between devices  16 us (5%)
  between operations  14.3 us (5%)
  local copies, waits for them, and re-layouts  6.62 us (2%)
  other arithmetic  6.08 us (2%)
    all_to_all x1, blocking collectives, body(): lax.all_to_all(outbound, 'expert', split_axis=1, concat_axis=1, tiled=True)  111 us
    reduce_scatter x1, waiting for transfers between devices, body(): lax.psum_scatter(out_part, 'tensor', scatter_dimension=2, tiled=True)  51.9 us
    reduce_scatter x1, waiting for transfers between devices, body(): lax.psum_scatter(input_part, 'tensor', scatter_dimension=2, tiled=True)  39.2 us
    all_to_all x1, waiting for transfers between devices, body(): blocks = lax.all_to_all(blocks, 'tensor', split_axis=0, concat_axis=0)  13.1 us
    all_to_all x1, starting transfers between devices, body(): lax.all_to_all(going_back, 'expert', split_axis=1, concat_axis=1, tiled=T...  10.4 us
    all_to_all x1, waiting for transfers between devices, body(): lax.all_to_all(going_back, 'expert', split_axis=1, concat_axis=1, tiled=T...  7.53 us
  transfers between devices with their start and end apart: 5, of which 5 were waited for; matrix products, arithmetic and copies ran while one was open for 5% of the time, Pallas kernels for 0%

profile of v1, /device:TPU:1, one launch (start us, length us, event | category | flops | bytes accessed | tf_op | source)
XLA Modules:
  0.0 292.6 jit_solution(17322614337723214446)
XLA Ops:
  8.1 1.0 fusion.24
  9.1 0.9 pad_maximum_fusion.1
  10.0 1.1 stack.28
  11.1 4.8 %all-to-all-start = ((bf16[4,2,128,512]{3,2,1,0:T(8,128)(2,1)}), bf16[4,2,128,512]{3,2,1,0:T(8,128)(2,1)S(1)}, u32[]{:S(2)}, u32[]{:S(2)}) async-start(bf16[4,2,128,512]{3,2,1,0:T(8,128)(2,1)} %stack.28), calls=%async_computation | async-start | bytes 2097152 | tf_op jit(solution)/shard_map/all_to_all | solution.py:44
  16.1 13.1 %all-to-all-done = bf16[4,2,128,512]{3,2,1,0:T(8,128)(2,1)S(1)} async-done(((bf16[4,2,128,512]{3,2,1,0:T(8,128)(2,1)}), bf16[4,2,128,512]{3,2,1,0:T(8,128)(2,1)S(1)}, u32[]{:S(2)}, u32[]{:S(2)}) %all-to-all-start) | async-done | bytes 1048608 | tf_op jit(solution)/shard_map/all_to_all | solution.py:44
  29.3 1.3 convert_bitcast_fusion
  31.2 110.6 %all_to_all.15 = bf16[2,64,8,2048]{3,2,0,1:T(8,128)(2,1)S(1)} all-to-all(bf16[2,64,8,2048]{3,2,0,1:T(8,128)(2,1)S(1)} %copy.30), channel_id=1, replica_groups=mesh['expert'=64,'tensor'=4] {'expert'}, dimensions={1} | all-to-all | bytes 8388608 | tf_op jit(solution)/shard_map/all_to_all | solution.py:55
  141.8 1.2 fusion.12
  143.0 1.9 copy-done.5
  144.9 1.3 fusion.5
  146.2 1.6 multiply_convert_fusion.2
  147.9 1.3 fusion.10
  149.2 3.3 %add_bitcast_fusion = f32[64,8,2048]{2,1,0:T(8,128)} fusion(f32[512,2048]{1,0:T(8,128)S(1)} %fusion.10, bf16[512,512]{1,0:T(8,128)(2,1)S(1)} %get-tuple-element.27, bf16[1,2048,512]{2,1,0:T(8,128)(2,1)S(1)} %copy-done), kind=kOutput, calls=%fused_computation | convolution fusion | flops 1074790400 | bytes 11010048 | tf_op jit(solution)/shard_map/dot_general | solution.py:88
  152.5 4.8 %fusion.3 = f32[64,8,2048]{2,1,0:T(8,128)} fusion(bf16[1,512,2048]{2,1,0:T(8,128)(2,1)} %param.15, bf16[512,512]{1,0:T(8,128)(2,1)S(1)} %get-tuple-element.25), kind=kOutput, calls=%fused_computation.12 | convolution fusion | flops 1073741824 | bytes 6815744 | tf_op jit(solution)/shard_map/dot_general | solution.py:69
  157.4 39.2 %reduce-scatter.5.cloned.1.call-done = f32[64,8,512]{2,1,0:T(8,128)} async-done(((f32[64,8,2048]{2,1,0:T(8,128)}), f32[64,8,512]{2,1,0:T(8,128)}) %reduce-scatter.5.cloned.1.call-update) | async-done | bytes 1048592 | tf_op jit(solution)/shard_map/reduce_scatter | solution.py:93
  196.6 51.9 %reduce-scatter.3.cloned.1.call-done = f32[64,8,512]{2,1,0:T(8,128)} async-done(((f32[64,8,2048]{2,1,0:T(8,128)}), f32[64,8,512]{2,1,0:T(8,128)}) %reduce-scatter.3.cloned.1.call-update) | async-done | bytes 1048592 | tf_op jit(solution)/shard_map/reduce_scatter | solution.py:92
  248.5 2.8 broadcast_select_fusion
  252.0 2.3 collective-permute-done
  254.7 1.0 copy.31
  255.7 10.4 %all-to-all-start.2 = ((bf16[2,64,4,512]{3,2,0,1:T(4,128)(2,1)}), bf16[2,64,4,512]{3,2,0,1:T(4,128)(2,1)S(1)}, u32[]{:S(2)}, u32[]{:S(2)}) async-start(bf16[2,64,4,512]{3,2,0,1:T(4,128)(2,1)} %copy.31), calls=%async_computation.4 | async-start | bytes 1048576 | tf_op jit(solution)/shard_map/all_to_all | solution.py:100
  266.1 4.5 %fusion.2 = bf16[1,512,2048]{2,1,0:T(8,128)(2,1)} fusion(bf16[512,512]{1,0:T(8,128)(2,1)} %copy-done.9, bf16[2,64,8,2048]{3,2,0,1:T(8,128)(2,1)} %copy-done.1), kind=kOutput, calls=%fused_computation.7 | convolution fusion | flops 1074790400 | bytes 4718592 | tf_op jit(solution)/shard_map/dot_general | solution.py:83
  270.6 2.6 fusion
  273.2 2.6 fusion.1
  275.9 7.5 %all-to-all-done.2 = bf16[2,64,4,512]{3,2,0,1:T(4,128)(2,1)S(1)} async-done(((bf16[2,64,4,512]{3,2,0,1:T(4,128)(2,1)}), bf16[2,64,4,512]{3,2,0,1:T(4,128)(2,1)S(1)}, u32[]{:S(2)}, u32[]{:S(2)}) %all-to-all-start.2) | async-done | bytes 524320 | tf_op jit(solution)/shard_map/all_to_all | solution.py:100
  (43 shorter events, 5.3 us)
Async XLA Ops:
  7.2 139.0 %copy-start = (bf16[1,2048,512]{2,1,0:T(8,128)(2,1)S(1)}, bf16[1,2048,512]{2,1,0:T(8,128)(2,1)}, u32[]{:S(2)}) copy-start(bf16[1,2048,512]{2,1,0:T(8,128)(2,1)} %param.14) | copy-start | bytes 6291460
  8.1 7.9 %copy-start.12 = (s32[128,1]{0,1:T(1,128)S(1)}, s32[128,1]{0,1:T(1,128)}, u32[]{:S(2)}) copy-start(s32[128,1]{0,1:T(1,128)} %param.9) | copy-start | bytes 1540
  11.1 18.1 %all-to-all-start = ((bf16[4,2,128,512]{3,2,1,0:T(8,128)(2,1)}), bf16[4,2,128,512]{3,2,1,0:T(8,128)(2,1)S(1)}, u32[]{:S(2)}, u32[]{:S(2)}) async-start(bf16[4,2,128,512]{3,2,1,0:T(8,128)(2,1)} %stack.28), calls=%async_computation | async-start | bytes 2097152 | tf_op jit(solution)/shard_map/all_to_all | solution.py:44
  15.9 180.7 %reduce-scatter.5.cloned.1.call-start = ((), (), s32[]{:S(2)}) async-start(), calls=%async_computation.6 | async-start | bytes 5242880 | tf_op jit(solution)/shard_map/reduce_scatter | solution.py:93
  31.2 110.6 %copy-start.6 = (bf16[1,2048,512]{2,1,0:T(8,128)(2,1)S(1)}, bf16[1,2048,512]{2,1,0:T(8,128)(2,1)}, u32[]{:S(2)}) copy-start(bf16[1,2048,512]{2,1,0:T(8,128)(2,1)} %param.13) | copy-start | bytes 6291460
  141.8 4.4 %copy-start.1 = (bf16[2,64,8,2048]{3,2,0,1:T(8,128)(2,1)}, bf16[2,64,8,2048]{3,2,0,1:T(8,128)(2,1)S(1)}, u32[]{:S(2)}) copy-start(bf16[2,64,8,2048]{3,2,0,1:T(8,128)(2,1)S(1)} %all_to_all.15) | copy-start | bytes 12582916
  141.8 3.1 %copy-start.5 = (bf16[1,512,2048]{2,1,0:T(8,128)(2,1)S(1)}, bf16[1,512,2048]{2,1,0:T(8,128)(2,1)}, u32[]{:S(2)}) copy-start(bf16[1,512,2048]{2,1,0:T(8,128)(2,1)} %param.15) | copy-start | bytes 6291460
  147.8 1.3 copy-start.7
  147.9 1.3 copy-start.10
  147.9 4.7 %copy-start.9 = (bf16[512,512]{1,0:T(8,128)(2,1)}, bf16[512,512]{1,0:T(8,128)(2,1)S(1)}, u32[]{:S(2)}) copy-start(bf16[512,512]{1,0:T(8,128)(2,1)S(1)} %get-tuple-element.25) | copy-start | bytes 1572868
  152.5 96.0 %reduce-scatter.3.cloned.1.call-start = ((), (), s32[]{:S(2)}) async-start(), calls=%async_computation.5 | async-start | bytes 5242880 | tf_op jit(solution)/shard_map/reduce_scatter | solution.py:92
  196.6 57.7 %copy-start.3 = (f32[64,8,512]{2,1,0:T(8,128)S(1)}, f32[64,8,512]{2,1,0:T(8,128)}, u32[]{:S(2)}) copy-start(f32[64,8,512]{2,1,0:T(8,128)} %reduce-scatter.5.cloned.1.call-done) | copy-start | bytes 3145732
  248.5 5.8 %copy-start.4 = (f32[64,8,512]{2,1,0:T(8,128)S(1)}, f32[64,8,512]{2,1,0:T(8,128)}, u32[]{:S(2)}) copy-start(f32[64,8,512]{2,1,0:T(8,128)} %reduce-scatter.3.cloned.1.call-done) | copy-start | bytes 3145732
  251.3 3.0 %collective-permute-start = (f32[2,64,4,512]{3,2,1,0:T(4,128)S(1)}, f32[2,64,4,512]{3,2,1,0:T(4,128)S(1)}, u32[]{:S(2)}, u32[]{:S(2)}) collective-permute-start(f32[2,64,4,512]{3,2,1,0:T(4,128)S(1)} %broadcast_select_fusion), channel_id=1, source_target_pairs={{0,4},{4,0},{8,12},{12,8},{16,20},{20,16},{24,28},{28,24},{32,36},... | collective-permute-start | bytes 3145736 | tf_op jit(solution)/shard_map/ppermute | solution.py:10
  255.7 27.7 %all-to-all-start.2 = ((bf16[2,64,4,512]{3,2,0,1:T(4,128)(2,1)}), bf16[2,64,4,512]{3,2,0,1:T(4,128)(2,1)S(1)}, u32[]{:S(2)}, u32[]{:S(2)}) async-start(bf16[2,64,4,512]{3,2,0,1:T(4,128)(2,1)} %copy.31), calls=%async_computation.4 | async-start | bytes 1048576 | tf_op jit(solution)/shard_map/all_to_all | solution.py:100
  266.1 4.5 %copy-start.2 = (bf16[2,64,8,2048]{3,2,0,1:T(8,128)(2,1)S(1)}, bf16[2,64,8,2048]{3,2,0,1:T(8,128)(2,1)}, u32[]{:S(2)}) copy-start(bf16[2,64,8,2048]{3,2,0,1:T(8,128)(2,1)} %copy-done.1) | copy-start | bytes 12582916
  266.1 4.5 %copy-start.8 = (bf16[512,512]{1,0:T(8,128)(2,1)S(1)}, bf16[512,512]{1,0:T(8,128)(2,1)}, u32[]{:S(2)}) copy-start(bf16[512,512]{1,0:T(8,128)(2,1)} %copy-done.7) | copy-start | bytes 1572868
  270.6 2.6 copy-start.11
Sparse Core Ops, SparseCore 0:
  152.6 43.9 reduce-scatter.4
  199.3 49.1 reduce-scatter.2
